TPU v7x, 256 devices: a whole 4x4x8 slice. The times are simulated.
256 devices in a mesh: row: 16 (over x, y_hi, core), col: 16 (over y_lo, z).
Axes of the slice: x: 4, y: 4 (y_hi: 2, y_lo: 2; y = y_hi * 2 + y_lo), z: 8, core: 2. Of those that a mesh axis runs over, the one named last changes fastest.
Arguments:
- left_rows: float32 [1024, 61440], P('col', 'row'), may hold values from -1.2 to 1.2
- right_cols: float32 [61440, 4096], P('col', 'row'), may hold values from -1.2 to 1.2
- left_pattern: int32 [16, 240], replicated, may hold values from 0 to 1, as said below
- right_pattern: int32 [240, 16], replicated, may hold values from 0 to 1, as said below
Outputs:
- square_terms: float32 [1024, 4096], P('col', 'row')
Inputs may be any that keep to these rules, and one draw needn't show every extreme that they name: Every device's tile of left_pattern (row b, inner blocks from a * 15) has between 1 and 3 occupied blocks, and some tile has exactly 3 in every draw. Every device's tile of right_pattern (inner blocks from b * 15, column a) has between 1 and 3 occupied blocks, and some tile has exactly 3 in every draw.
All inputs are finite; a program needn't handle non-finite values.
Results may differ from a plain program's by a relative error of at most 0.0001.
Values sent between devices are 32-bit elements; how exact they have to be, the bound alone decides.
No kernel may reach another device: no remote copies, remote signals or barrier semaphores. Data moves between devices by JAX's collectives and lax.ppermute only.
A program may use at most 128 MiB of HBM per device.

v0:
```python
import jax
import jax.numpy as jnp
from jax import lax
from jax.sharding import PartitionSpec as P

STEPS = 4
CAP = 3


def from_behind(value, axis, steps):
    count = lax.axis_size(axis)
    pairs = [(source, (source - steps) % count) for source in range(count)]
    return lax.ppermute(value, axis, pairs)


def occupied(flags, cap):
    flags = flags != 0
    rank = jnp.cumsum(flags.astype(jnp.int32)) - 1
    where = jnp.arange(flags.shape[0], dtype=jnp.int32)
    hit = flags[None, :] & (rank[None, :] == jnp.arange(cap, dtype=jnp.int32)[:, None])
    index = jnp.sum(jnp.where(hit, where[None, :], 0), axis=1)
    return (index, jnp.any(hit, axis=1))


def left_flags(left_pattern, block_row, block_col, per_k):
    return lax.dynamic_slice(left_pattern, (block_row, block_col * per_k), (1, per_k)).reshape(-1)


def right_flags(right_pattern, block_row, block_col, trows):
    return lax.dynamic_slice(right_pattern, (block_row * trows, block_col), (trows, 1)).reshape(-1)


def pick_cols(x, index, blk):
    return jnp.concatenate(
        [lax.dynamic_slice_in_dim(x, index[s] * blk, blk, axis=1) for s in range(index.shape[0])],
        axis=1,
    )


def pick_rows(x, index, blk):
    return jnp.concatenate(
        [lax.dynamic_slice_in_dim(x, index[s] * blk, blk, axis=0) for s in range(index.shape[0])],
        axis=0,
    )


def body(left_rows, right_cols, left_pattern, right_pattern):
    nrow = lax.axis_size("row")
    ncol = lax.axis_size("col")
    ratio = nrow // ncol
    lrows, left_width = left_rows.shape
    right_height, blk = right_cols.shape
    per_k = left_width // blk
    trows = right_height // blk
    rowdev = lax.axis_index("row")
    coldev = lax.axis_index("col")
    own_left, _ = occupied(left_flags(left_pattern, coldev, rowdev, per_k), CAP)
    own_right, _ = occupied(right_flags(right_pattern, coldev, rowdev, trows), CAP)
    left_small = pick_cols(left_rows, own_left, blk)
    right_small = pick_rows(right_cols, own_right, blk)
    roots = [(coldev * ratio + step) % nrow for step in range(STEPS)]
    slots = jnp.stack(
        [jnp.where(rowdev == root, left_small, jnp.zeros_like(left_small)) for root in roots]
    )
    lefts = lax.psum(slots, "row")
    total = jnp.zeros((lrows, blk), jnp.float32)
    highest = lax.Precision.HIGHEST
    for step in range(STEPS):
        shift = step // ratio
        right = right_small if shift == 0 else from_behind(right_small, "col", shift)
        panel = roots[step]
        lidx, lok = occupied(left_flags(left_pattern, coldev, panel, per_k), CAP)
        ridx, rok = occupied(
            right_flags(right_pattern, (coldev + shift) % ncol, rowdev, trows), CAP
        )
        match = ((lidx[:, None] == ridx[None, :]) & lok[:, None] & rok[None, :]).astype(jnp.float32)
        left = lefts[step]
        blocks = [left[:, i * blk : (i + 1) * blk] for i in range(CAP)]
        aligned = []
        for j in range(CAP):
            part = match[0, j] * blocks[0]
            for i in range(1, CAP):
                part = part + match[i, j] * blocks[i]
            aligned.append(part)
        aligned = jnp.concatenate(aligned, axis=1)
        total = total + jnp.dot(
            aligned, right, precision=highest, preferred_element_type=jnp.float32
        )
    return total


def solution(mesh):
    return jax.shard_map(
        body,
        mesh=mesh,
        in_specs=(P("col", "row"), P("col", "row"), P(), P()),
        out_specs=P("col", "row"),
        check_vma=False,
    )
```

profile of v0, /device:TPU:1, one launch (start us, length us, event | category | flops | bytes accessed | tf_op | source)
XLA Modules:
  0.0 217.3 jit_solution(2198795887849036355)
XLA Ops:
  6.5 1.0 compare_bitcast_fusion.3
  7.7 1.0 compare_bitcast_fusion.2
  8.7 0.2 reduce-window.83
  9.0 0.7 fusion.55
  11.7 1.2 constant_dynamic-slice_fusion.2
  12.9 7.5 %collective-permute-start = (f32[768,256]{1,0:T(8,128)S(1)}, f32[768,256]{1,0:T(8,128)S(1)}, u32[]{:S(2)}, u32[]{:S(2)}) collective-permute-start(f32[768,256]{1,0:T(8,128)S(1)} %pad_maximum_fusion.1), channel_id=1, source_target_pairs={{0,15},{1,0},{2,1},{3,2},{4,3},{5,4},{6,5},{7,6},{8,7},{9,8},{10,9... | collective-permute-start | bytes 2359304 | tf_op jit(solution)/shard_map/ppermute | solution.py:13
  20.4 1.6 collective-permute-start.2
  22.0 0.6 fusion.54
  24.6 0.9 dynamic-slice_bitcast_fusion.2
  25.6 0.9 pad_maximum_fusion
  26.6 0.2 reduce-window.84
  26.8 0.2 reduce-window.80
  27.0 0.2 reduce-window.85
  27.2 0.2 reduce-window.81
  28.0 0.2 reduce-window.88
  28.2 0.2 reduce-window.86
  28.4 0.2 reduce-window.87
  28.6 0.2 reduce-window.89
  29.3 0.7 fusion.50
  30.2 0.7 fusion.51
  31.0 0.7 fusion.52
  31.7 0.7 fusion.53
  32.4 150.2 %all-reduce.2.cloned.1.call-done = f32[4,64,768]{2,1,0:T(8,128)} async-done(((f32[4,64,768]{2,1,0:T(8,128)}), f32[4,64,768]{2,1,0:T(8,128)}) %all-reduce.2.cloned.1.call-update) | async-done | bytes 786448 | tf_op jit(solution)/shard_map/psum | solution.py:65
  182.6 1.3 slice_bitcast_fusion.1
  183.9 5.5 %multiply_add_fusion.5 = (f32[64,256]{1,0:T(8,128)S(1)}, f32[64,256]{1,0:T(8,128)S(1)}, f32[64,256]{1,0:T(8,128)S(1)}) fusion(f32[64,768]{1,0:T(8,128)S(1)} %get-tuple-element.11, f32[]{:T(128)} %bitcast.52, f32[]{:T(128)} %bitcast.51, f32[]{:T(128)} %bitcast.49, f32[]{:T(128)} %bitcast.55, f32[]{:T(128)} %bitcast.54, f32[]{:T(128)} %bitcast.53, ...), kind=kLoop, calls=%fused_computation.41 | loop fusion | flops 245760 | bytes 393252 | tf_op jit(solution)/shard_map/add | solution.py:83
  189.4 5.8 %multiply_add_fusion.8 = (f32[64,256]{1,0:T(8,128)S(1)}, f32[64,256]{1,0:T(8,128)S(1)}, f32[64,256]{1,0:T(8,128)S(1)}) fusion(f32[64,768]{1,0:T(8,128)S(1)} %get-tuple-element.13, f32[]{:T(128)} %bitcast.37, f32[]{:T(128)} %bitcast.36, f32[]{:T(128)} %bitcast.34, f32[]{:T(128)} %bitcast.40, f32[]{:T(128)} %bitcast.39, f32[]{:T(128)} %bitcast.38, ...), kind=kLoop, calls=%fused_computation.44 | loop fusion | flops 245760 | bytes 393252 | tf_op jit(solution)/shard_map/add | solution.py:83
  195.2 5.7 %multiply_add_fusion.11 = (f32[64,256]{1,0:T(8,128)S(1)}, f32[64,256]{1,0:T(8,128)S(1)}, f32[64,256]{1,0:T(8,128)S(1)}) fusion(f32[64,768]{1,0:T(8,128)S(1)} %get-tuple-element.14, f32[]{:T(128)} %bitcast.17, f32[]{:T(128)} %bitcast.16, f32[]{:T(128)} %bitcast.5, f32[]{:T(128)} %bitcast.20, f32[]{:T(128)} %bitcast.19, f32[]{:T(128)} %bitcast.18, ...), kind=kLoop, calls=%fused_computation.47 | loop fusion | flops 245760 | bytes 393252 | tf_op jit(solution)/shard_map/add | solution.py:83
  201.0 0.5 fusion.1
  201.5 5.6 %multiply_add_fusion.2 = (f32[64,256]{1,0:T(8,128)S(1)}, f32[64,256]{1,0:T(8,128)S(1)}, f32[64,256]{1,0:T(8,128)S(1)}) fusion(f32[64,768]{1,0:T(8,128)S(1)} %get-tuple-element.12, f32[]{:T(128)} %bitcast.67, f32[]{:T(128)} %bitcast.66, f32[]{:T(128)} %bitcast.64, f32[]{:T(128)} %bitcast.70, f32[]{:T(128)} %bitcast.69, f32[]{:T(128)} %bitcast.68, ...), kind=kLoop, calls=%fused_computation.38 | loop fusion | flops 245760 | bytes 393252 | tf_op jit(solution)/shard_map/add | solution.py:83
  207.1 1.6 fusion.17
  208.7 0.5 convolution_add_fusion.1
  209.3 1.1 fusion
  (32 shorter events, 2.1 us)
Async XLA Ops:
  6.5 176.1 %all-reduce.2.cloned.1.call-start = ((), (), s32[]{:S(2)}) async-start(), calls=%async_computation | async-start | bytes 1572864 | tf_op jit(solution)/shard_map/psum | solution.py:65
  12.9 195.8 %collective-permute-start = (f32[768,256]{1,0:T(8,128)S(1)}, f32[768,256]{1,0:T(8,128)S(1)}, u32[]{:S(2)}, u32[]{:S(2)}) collective-permute-start(f32[768,256]{1,0:T(8,128)S(1)} %pad_maximum_fusion.1), channel_id=1, source_target_pairs={{0,15},{1,0},{2,1},{3,2},{4,3},{5,4},{6,5},{7,6},{8,7},{9,8},{10,9... | collective-permute-start | bytes 2359304 | tf_op jit(solution)/shard_map/ppermute | solution.py:13
  20.4 186.7 %collective-permute-start.2 = (f32[768,256]{1,0:T(8,128)S(1)}, f32[768,256]{1,0:T(8,128)}, u32[]{:S(2)}, u32[]{:S(2)}) collective-permute-start(f32[768,256]{1,0:T(8,128)S(1)} %pad_maximum_fusion.1), channel_id=1, source_target_pairs={{0,13},{1,14},{2,15},{3,0},{4,1},{5,2},{6,3},{7,4},{8,5},{9,6},{10... | collective-permute-start | bytes 2359304 | tf_op jit(solution)/shard_map/ppermute | solution.py:13
  22.0 187.3 %collective-permute-start.1 = (f32[768,256]{1,0:T(8,128)S(1)}, f32[768,256]{1,0:T(8,128)S(1)}, u32[]{:S(2)}, u32[]{:S(2)}) collective-permute-start(f32[768,256]{1,0:T(8,128)S(1)} %pad_maximum_fusion.1), channel_id=1, source_target_pairs={{0,14},{1,15},{2,0},{3,1},{4,2},{5,3},{6,4},{7,5},{8,6},{9,7},{10,... | collective-permute-start | bytes 2359304 | tf_op jit(solution)/shard_map/ppermute | solution.py:13
Sparse Core Ops, SparseCore 0:
  26.7 155.8 all-reduce.1
where the time goes:
time: 218 us; the launch traced here: 217 us
  waiting for transfers between devices  150 us (69%)
  other arithmetic  29.2 us (13%)
  between operations  17.4 us (8%)
  starting transfers between devices  9.11 us (4%)
  local copies, waits for them, and re-layouts  7.41 us (3%)
  matrix products  3.81 us (2%)
    psum x1, waiting for transfers between devices, body(): lefts = lax.psum(slots, 'row')  150 us
    add x4, other arithmetic, body(): part = part + match[i, j] * blocks[i]  22.6 us
    ppermute x3, starting transfers between devices, from_behind(): return lax.ppermute(value, axis, pairs)  9.11 us
  transfers between devices with their start and end apart: 4, of which 1 were waited for; matrix products, arithmetic and copies ran while one was open for 16% of the time, Pallas kernels for 0%

commit v1 on v0

--- a/solution.py
+++ b/solution.py
@@ -62,7 +62,7 @@
     slots = jnp.stack(
         [jnp.where(rowdev == root, left_small, jnp.zeros_like(left_small)) for root in roots]
     )
-    lefts = lax.psum(slots, "row")
+    lefts = jnp.sum(lax.all_gather(slots, "row"), axis=0)
     total = jnp.zeros((lrows, blk), jnp.float32)
     highest = lax.Precision.HIGHEST
     for step in range(STEPS):

time: 218 us -> 187 us (0.86)
  the two profiles are of different devices: /device:TPU:1 before, /device:TPU:225 now
where the time goes in v1:
time: 187 us; the launch traced here: 186 us
  waiting for transfers between devices  121 us (65%)
  other arithmetic  34.8 us (19%)
  between operations  17.4 us (9%)
  local copies, waits for them, and re-layouts  6.26 us (3%)
  matrix products  4.94 us (3%)
  starting transfers between devices  1.96 us (1%)
    all_gather x1, waiting for transfers between devices, body(): lefts = jnp.sum(lax.all_gather(slots, 'row'), axis=0)  121 us
    add x4, other arithmetic, body(): part = part + match[i, j] * blocks[i]  22.8 us
    reduce_sum x1, other arithmetic, body(): lefts = jnp.sum(lax.all_gather(slots, 'row'), axis=0)  5.43 us
    dot_general x4, matrix products, body(): jnp.dot(aligned, right, precision=highest, preferred_element_type=jnp.flo...  4.94 us
  transfers between devices with their start and end apart: 4, of which 1 were waited for; matrix products, arithmetic and copies ran while one was open for 21% of the time, Pallas kernels for 0%

profile of v1, /device:TPU:225, one launch (start us, length us, event | category | flops | bytes accessed | tf_op | source)
XLA Modules:
  0.0 186.2 jit_solution(14499521365751892398)
XLA Ops:
  6.5 0.9 compare_bitcast_fusion.3
  7.5 0.2 reduce-window.82
  7.7 0.9 compare_bitcast_fusion.2
  8.6 0.2 reduce-window.83
  9.0 0.7 fusion.54
  11.7 0.9 dynamic-slice_bitcast_fusion.2
  12.7 0.9 pad_maximum_fusion
  13.6 0.7 fusion.55
  16.2 1.2 constant_dynamic-slice_fusion.2
  17.4 0.8 collective-permute-start
  18.3 0.9 collective-permute-start.2
  19.2 0.2 collective-permute-start.1
  19.4 0.2 reduce-window.88
  19.6 0.2 reduce-window.86
  19.8 0.2 reduce-window.87
  20.0 0.2 reduce-window.89
  20.1 0.2 reduce-window.84
  20.7 0.2 reduce-window.81
  22.3 0.7 fusion.50
  23.0 0.7 fusion.51
  23.8 0.7 fusion.52
  24.5 0.7 fusion.53
  25.2 120.8 %all-gather.3.cloned.1.call-done = f32[64,64,768]{2,1,0:T(8,128)} async-done(((f32[4,64,768]{2,1,0:T(8,128)}), f32[64,64,768]{2,1,0:T(8,128)}) %all-gather.3.cloned.1.call-update) | async-done | bytes 12582928 | tf_op jit(solution)/shard_map/all_gather | solution.py:65
  146.0 5.4 %reduce_sum.102 = f32[4,64,768]{2,1,0:T(8,128)S(1)} reduce(f32[16,4,64,768]{3,2,1,0:T(8,128)} %bitcast.110, f32[]{:T(128)} %constant.86.clone.1), dimensions={0}, to_apply=%region_8.9 | reduce | flops 2949120 | bytes 13369348 | tf_op jit(solution)/shard_map/reduce_sum | solution.py:65
  151.5 5.7 %multiply_add_fusion.5 = (f32[64,256]{1,0:T(8,128)S(1)}, f32[64,256]{1,0:T(8,128)S(1)}, f32[64,256]{1,0:T(8,128)S(1)}) fusion(f32[64,768]{1,0:T(8,128)S(1)} %get-tuple-element.11, f32[]{:T(128)} %bitcast.53, f32[]{:T(128)} %bitcast.52, f32[]{:T(128)} %bitcast.50, f32[]{:T(128)} %bitcast.56, f32[]{:T(128)} %bitcast.55, f32[]{:T(128)} %bitcast.54, ...), kind=kLoop, calls=%fused_computation.41 | loop fusion | flops 245760 | bytes 393252 | tf_op jit(solution)/shard_map/add | solution.py:83
  157.2 5.7 %multiply_add_fusion.8 = (f32[64,256]{1,0:T(8,128)S(1)}, f32[64,256]{1,0:T(8,128)S(1)}, f32[64,256]{1,0:T(8,128)S(1)}) fusion(f32[64,768]{1,0:T(8,128)S(1)} %get-tuple-element.13, f32[]{:T(128)} %bitcast.38, f32[]{:T(128)} %bitcast.37, f32[]{:T(128)} %bitcast.35, f32[]{:T(128)} %bitcast.41, f32[]{:T(128)} %bitcast.40, f32[]{:T(128)} %bitcast.39, ...), kind=kLoop, calls=%fused_computation.44 | loop fusion | flops 245760 | bytes 393252 | tf_op jit(solution)/shard_map/add | solution.py:83
  162.9 5.7 %multiply_add_fusion.11 = (f32[64,256]{1,0:T(8,128)S(1)}, f32[64,256]{1,0:T(8,128)S(1)}, f32[64,256]{1,0:T(8,128)S(1)}) fusion(f32[64,768]{1,0:T(8,128)S(1)} %get-tuple-element.14, f32[]{:T(128)} %bitcast.18, f32[]{:T(128)} %bitcast.17, f32[]{:T(128)} %bitcast.5, f32[]{:T(128)} %bitcast.21, f32[]{:T(128)} %bitcast.20, f32[]{:T(128)} %bitcast.19, ...), kind=kLoop, calls=%fused_computation.47 | loop fusion | flops 245760 | bytes 393252 | tf_op jit(solution)/shard_map/add | solution.py:83
  168.6 0.5 fusion.1
  169.2 5.7 %multiply_add_fusion.2 = (f32[64,256]{1,0:T(8,128)S(1)}, f32[64,256]{1,0:T(8,128)S(1)}, f32[64,256]{1,0:T(8,128)S(1)}) fusion(f32[64,768]{1,0:T(8,128)S(1)} %get-tuple-element.12, f32[]{:T(128)} %bitcast.68, f32[]{:T(128)} %bitcast.67, f32[]{:T(128)} %bitcast.65, f32[]{:T(128)} %bitcast.71, f32[]{:T(128)} %bitcast.70, f32[]{:T(128)} %bitcast.69, ...), kind=kLoop, calls=%fused_computation.38 | loop fusion | flops 245760 | bytes 393252 | tf_op jit(solution)/shard_map/add | solution.py:83
  174.9 1.6 fusion.17
  176.6 1.6 convolution_add_fusion.1
  178.2 1.1 fusion
  (33 shorter events, 2.3 us)
Async XLA Ops:
  6.5 139.5 %all-gather.3.cloned.1.call-start = ((), (), s32[]{:S(2)}) async-start(), calls=%async_computation | async-start | bytes 13369344 | tf_op jit(solution)/shard_map/all_gather | solution.py:65
  17.4 159.1 %collective-permute-start = (f32[768,256]{1,0:T(8,128)S(1)}, f32[768,256]{1,0:T(8,128)}, u32[]{:S(2)}, u32[]{:S(2)}) collective-permute-start(f32[768,256]{1,0:T(8,128)S(1)} %pad_maximum_fusion.1), channel_id=1, source_target_pairs={{0,15},{1,0},{2,1},{3,2},{4,3},{5,4},{6,5},{7,6},{8,7},{9,8},{10,9... | collective-permute-start | bytes 2359304 | tf_op jit(solution)/shard_map/ppermute | solution.py:13
  18.3 156.6 %collective-permute-start.2 = (f32[768,256]{1,0:T(8,128)S(1)}, f32[768,256]{1,0:T(8,128)}, u32[]{:S(2)}, u32[]{:S(2)}) collective-permute-start(f32[768,256]{1,0:T(8,128)S(1)} %pad_maximum_fusion.1), channel_id=1, source_target_pairs={{0,13},{1,14},{2,15},{3,0},{4,1},{5,2},{6,3},{7,4},{8,5},{9,6},{10... | collective-permute-start | bytes 2359304 | tf_op jit(solution)/shard_map/ppermute | solution.py:13
  19.2 159.0 %collective-permute-start.1 = (f32[768,256]{1,0:T(8,128)S(1)}, f32[768,256]{1,0:T(8,128)S(1)}, u32[]{:S(2)}, u32[]{:S(2)}) collective-permute-start(f32[768,256]{1,0:T(8,128)S(1)} %pad_maximum_fusion.1), channel_id=1, source_target_pairs={{0,14},{1,15},{2,0},{3,1},{4,2},{5,3},{6,4},{7,5},{8,6},{9,7},{10,... | collective-permute-start | bytes 2359304 | tf_op jit(solution)/shard_map/ppermute | solution.py:13
Sparse Core Ops, SparseCore 0:
  13.7 132.2 all-gather.2
